TPU v7x, 32 devices: a whole 2x2x4 slice. The times are simulated.
32 devices in a mesh: dp: 8 (over y, x, core), tensor: 4 (over z).
Axes of the slice: x: 2, y: 2, z: 4, core: 2. Of those that a mesh axis runs over, the one named last changes fastest.
Arguments:
- acts: bfloat16 [4096, 2048], P('dp', 'tensor'), may hold values from -6 to 6
- out_grads: bfloat16 [4096, 8192], P('dp', 'tensor'), may hold values from -6 to 6
- basis_out: bfloat16 [8192, 8192], P('tensor'), may hold values from -0.0625 to 0.0625
- basis_in: bfloat16 [2048, 2048], P('tensor'), may hold values from -0.125 to 0.125
- slot_sequence: int32 [16], replicated, may hold values from 0 to 15, each once
- seq_lengths: int32 [16], replicated, may hold values from 1 to 256, 2560 in all
Outputs:
- eigenvalues: float32 [8192, 2048], P('tensor', 'dp')
Inputs may be any that keep to these rules, and one draw needn't show every extreme that they name: `slot_sequence`: every sequence number appears exactly once. `seq_lengths`: the largest count is exactly 256.
All inputs are finite; a program needn't handle non-finite values.
Results may differ from a plain program's by a relative error of at most 0.0018.
Values may be sent and summed in bfloat16 or wider, within the bound.
No kernel may reach another device: no remote copies, remote signals or barrier semaphores. Data moves between devices by JAX's collectives and lax.ppermute only.
A program may use at most 128 MiB of HBM per device.

v0:
```python
import jax
import jax.numpy as jnp
from jax import lax
from jax.sharding import PartitionSpec as P

LEN = 256


def shards(acts, out_grads, basis_out, basis_in, slot_sequence, seq_lengths):
    tok_rows = acts.shape[0]
    local_seqs = tok_rows // LEN
    seq_total = seq_lengths.shape[0]
    group_index = lax.axis_index("dp")
    slot_ids = group_index * local_seqs + jnp.arange(local_seqs, dtype=jnp.int32)
    seq_numbers = jnp.arange(seq_total, dtype=jnp.int32)
    which_seq = jnp.sum(
        jnp.where(slot_ids[:, None] == seq_numbers[None, :], slot_sequence[None, :], 0), axis=1
    )
    slot_counts = jnp.sum(
        jnp.where(which_seq[:, None] == seq_numbers[None, :], seq_lengths[None, :], 0), axis=1
    )
    row_counts = jnp.repeat(slot_counts, LEN)
    positions = jnp.arange(tok_rows, dtype=jnp.int32) % LEN
    valid_mask = positions < row_counts
    masked = jnp.where(valid_mask[:, None], out_grads, jnp.zeros_like(out_grads))
    rot_sums = lax.psum_scatter(
        jnp.einsum("oi,to->it", basis_out, masked, preferred_element_type=jnp.float32),
        "tensor",
        scatter_dimension=0,
        tiled=True,
    )
    rot_grads = rot_sums.astype(jnp.bfloat16)
    whole_acts = lax.all_gather(acts, "tensor", axis=1, tiled=True)
    rot_acts = jnp.dot(
        whole_acts,
        lax.all_gather(basis_in, "tensor", axis=0, tiled=True),
        preferred_element_type=jnp.float32,
    ).astype(jnp.bfloat16)
    squares = jnp.zeros((rot_grads.shape[0], rot_acts.shape[1]), jnp.float32)
    for slot_pos in range(local_seqs):
        grad_slot = rot_grads[:, slot_pos * LEN : (slot_pos + 1) * LEN]
        act_slot = rot_acts[slot_pos * LEN : (slot_pos + 1) * LEN]
        rotated = jnp.dot(grad_slot, act_slot, preferred_element_type=jnp.float32)
        squares = squares + rotated * rotated
    summed = lax.psum_scatter(squares, "dp", scatter_dimension=1, tiled=True)
    return summed / (seq_total * LEN)


def solution(mesh):
    return jax.shard_map(
        shards,
        mesh=mesh,
        in_specs=(
            P("dp", "tensor"),
            P("dp", "tensor"),
            P("tensor", None),
            P("tensor", None),
            P(),
            P(),
        ),
        out_specs=P("tensor", "dp"),
        check_vma=False,
    )
```

profile of v0, /device:TPU:0, one launch (start us, length us, event | category | flops | bytes accessed | tf_op | source)
XLA Modules:
  0.0 628.3 jit_solution(10822918368611207636)
XLA Ops:
  6.5 0.0 copy-start.2
  6.5 0.0 copy-start.3
  6.5 0.0 copy-start.1
  6.5 0.0 all-gather.3.cloned.1.call-start
  6.5 0.7 all-gather.3.cloned.1.call-update
  7.3 0.0 all-gather.5.cloned.1.call-start
  7.3 0.7 all-gather.5.cloned.1.call-update
  8.0 0.0 reduce-scatter.3.cloned.1.call-start
  8.1 0.0 copy-done.2
  8.1 0.2 fusion.12
  8.3 0.0 copy-done.3
  8.3 0.2 fusion.13
  8.5 0.1 broadcast_bitcast_fusion
  8.5 0.0 copy-done.1
  8.5 26.9 %convolution_bitcast_fusion = f32[8192,512]{0,1:T(8,128)} fusion(bf16[2048,8192]{1,0:T(8,128)(2,1)} %param.8, bf16[512,2048]{1,0:T(8,128)(2,1)S(1)} %copy-done.1, pred[512]{0:T(512)(128)(4,1)S(1)} %fusion.8), kind=kOutput, calls=%fused_computation.1 | convolution fusion | flops 17180917760 | bytes 52429312 | tf_op jit(solution)/shard_map/oi,to->it/dot_general | solution.py:27
  35.4 0.0 reduce-scatter.3.cloned.1.call-update
  35.5 0.2 reduce-scatter.5.cloned.1.call-start
  35.7 21.6 %all-gather.3.cloned.1.call-done = bf16[512,2048]{1,0:T(8,128)(2,1)} async-done(((bf16[512,512]{1,0:T(8,128)(2,1)}), bf16[512,2048]{1,0:T(8,128)(2,1)}) %all-gather.3.cloned.1.call-update) | async-done | bytes 2097168 | tf_op jit(solution)/shard_map/all_gather | solution.py:33
  57.3 150.0 %all-gather.5.cloned.1.call-done = bf16[2048,2048]{1,0:T(8,128)(2,1)} async-done(((bf16[512,2048]{1,0:T(8,128)(2,1)}), bf16[2048,2048]{1,0:T(8,128)(2,1)}) %all-gather.5.cloned.1.call-update) | async-done | bytes 8388624 | tf_op jit(solution)/shard_map/all_gather | solution.py:36
  207.3 9.8 %convolution_convert_fusion = bf16[512,2048]{1,0:T(8,128)(2,1)} fusion(bf16[512,2048]{1,0:T(8,128)(2,1)} %all-gather.3.cloned.1.call-done, bf16[2048,2048]{1,0:T(8,128)(2,1)} %all-gather.5.cloned.1.call-done), kind=kOutput, calls=%fused_computation.2 | convolution fusion | flops 4296015872 | bytes 12582912 | tf_op jit(solution)/shard_map/dot_general | solution.py:34
  217.2 271.2 %reduce-scatter.3.cloned.1.call-done = f32[2048,512]{0,1:T(8,128)} async-done(((f32[8192,512]{0,1:T(8,128)}), f32[2048,512]{0,1:T(8,128)}) %reduce-scatter.3.cloned.1.call-update) | async-done | bytes 4194320 | tf_op jit(solution)/shard_map/reduce_scatter | solution.py:26
  488.4 0.0 copy-start
  488.4 2.6 convert_element_type.6
  491.0 0.2 copy-done
  491.2 2.4 fusion.4
  493.6 8.3 %multiply_add_fusion = f32[2048,2048]{1,0:T(8,128)} fusion(f32[2048,2048]{1,0:T(8,128)S(1)} %fusion.4, bf16[512,2048]{1,0:T(8,128)(2,1)} %convolution_convert_fusion, bf16[2048,512]{0,1:T(8,128)(2,1)S(1)} %convert_element_type.6), kind=kOutput, calls=%fused_computation | convolution fusion | flops 2160066560 | bytes 35651584 | tf_op jit(solution)/shard_map/dot_general | solution.py:43
  501.9 0.0 reduce-scatter.5.cloned.1.call-update
  501.9 116.8 %reduce-scatter.5.cloned.1.call-done = f32[2048,256]{1,0:T(8,128)} async-done(((f32[2048,2048]{1,0:T(8,128)}), f32[2048,256]{1,0:T(8,128)}) %reduce-scatter.5.cloned.1.call-update) | async-done | bytes 2097168 | tf_op jit(solution)/shard_map/reduce_scatter | solution.py:45
  618.7 3.0 broadcast_multiply_fusion
  (3 shorter events, 0.0 us)
Async XLA Ops:
  6.5 1.5 copy-start.2
  6.5 1.7 copy-start.3
  6.5 2.0 copy-start.1
  6.5 50.8 %all-gather.3.cloned.1.call-start = ((), (), s32[]{:S(2)}) async-start(), calls=%async_computation.3 | async-start | bytes 2621440 | tf_op jit(solution)/shard_map/all_gather | solution.py:33
  7.3 200.1 %all-gather.5.cloned.1.call-start = ((), (), s32[]{:S(2)}) async-start(), calls=%async_computation.4 | async-start | bytes 10485760 | tf_op jit(solution)/shard_map/all_gather | solution.py:36
  8.0 480.3 %reduce-scatter.3.cloned.1.call-start = ((), (), s32[]{:S(2)}) async-start(), calls=%async_computation.2 | async-start | bytes 20971520 | tf_op jit(solution)/shard_map/reduce_scatter | solution.py:26
  35.5 583.3 %reduce-scatter.5.cloned.1.call-start = ((), (), s32[]{:S(2)}) async-start(), calls=%async_computation.5 | async-start | bytes 18874368 | tf_op jit(solution)/shard_map/reduce_scatter | solution.py:45
  488.4 2.9 copy-start
Sparse Core Ops, SparseCore 0:
  8.9 48.3 all-gather.2
  58.9 148.4 all-gather.4
  209.7 278.6 reduce-scatter.2
  502.1 116.6 reduce-scatter.4
where the time goes:
time: 628 us
  waiting for transfers between devices  561 us (89%)
  matrix products  47.4 us (8%)
  between operations  13.2 us (2%)
    reduce_scatter x1, waiting for transfers between devices, shards(): lax.psum_scatter(jnp.einsum('oi,to->it', basis_out, masked, preferred_ele...  271 us
    all_gather x1, waiting for transfers between devices, shards(): lax.all_gather(basis_in, 'tensor', axis=0, tiled=True)  150 us
    reduce_scatter x1, waiting for transfers between devices, shards(): summed = lax.psum_scatter(squares, 'dp', scatter_dimension=1, tiled=True)  117 us
    dot_general x1, matrix products, shards(): jnp.einsum('oi,to->it', basis_out, masked, preferred_element_type=jnp.flo...  26.9 us
    all_gather x1, waiting for transfers between devices, shards(): whole_acts = lax.all_gather(acts, 'tensor', axis=1, tiled=True)  21.6 us
  transfers between devices with their start and end apart: 4, of which 4 were waited for; matrix products, arithmetic and copies ran while one was open for 6% of the time, Pallas kernels for 0%

commit v1 on v0

--- a/solution.py
+++ b/solution.py
@@ -4,6 +4,28 @@
 from jax.sharding import PartitionSpec as P
 
 LEN = 256
+
+
+def push_sectors_over_axis(w_in, out_dim):
+    w_in = jnp.moveaxis(w_in, 0, out_dim)
+    v1 = w_in.shape
+    return w_in.reshape(*v1[:out_dim], v1[out_dim] * v1[out_dim + 1], *v1[out_dim + 2 :])
+
+
+def trace_the_zone(obj, mesh_ax, along_dim):
+    world = lax.axis_size(mesh_ax)
+    trail = [(pp, (pp + 1) % world) for pp in range(world)]
+    pages = [(u, t) for t, u in trail]
+    r1, val = ([], [])
+    for kk in range(world - 1):
+        if kk % 2 == 0:
+            r1.append(lax.ppermute(r1[-1] if r1 else obj, axis_name=mesh_ax, perm=trail))
+        else:
+            val.append(lax.ppermute(val[-1] if val else obj, perm=pages, axis_name=mesh_ax))
+    step_out = jnp.stack([*r1[::-1], obj, *val], axis=0)
+    raw_out = lax.axis_index(mesh_ax) - len(r1)
+    step_out = step_out[(jnp.arange(world) - raw_out) % world]
+    return push_sectors_over_axis(step_out, along_dim)
 
 
 def shards(acts, out_grads, basis_out, basis_in, slot_sequence, seq_lengths):
@@ -32,9 +54,7 @@
     rot_grads = rot_sums.astype(jnp.bfloat16)
     whole_acts = lax.all_gather(acts, "tensor", axis=1, tiled=True)
     rot_acts = jnp.dot(
-        whole_acts,
-        lax.all_gather(basis_in, "tensor", axis=0, tiled=True),
-        preferred_element_type=jnp.float32,
+        whole_acts, trace_the_zone(basis_in, "tensor", 0), preferred_element_type=jnp.float32
     ).astype(jnp.bfloat16)
     squares = jnp.zeros((rot_grads.shape[0], rot_acts.shape[1]), jnp.float32)
     for slot_pos in range(local_seqs):

time: 628 us -> 605 us (0.963)
  waiting for transfers between devices: 561 us -> 501 us
  local copies, waits for them, and re-layouts: 0.29 us -> 16.6 us
  other arithmetic: 6.06 us -> 19.5 us
    ppermute x0 -> x3, waiting for transfers between devices: none -> 223 us  [the longest x1 115 us: trace_the_zone(): lax.ppermute(val[-1] if val else obj, perm=pages, axis_name=mesh_ax)]
    all_gather x1 -> x0, waiting for transfers between devices: 150 us -> none  [shards(): lax.all_gather(basis_in, 'tensor', axis=0, tiled=True)]
    reduce_scatter x1, waiting for transfers between devices: 271 us -> 160 us  [shards(): lax.psum_scatter(jnp.einsum('oi,to->it', basis_out, masked, preferred_ele...]
    all_gather x1, waiting for transfers between devices: 21.6 us -> 0.01 us  [shards(): whole_acts = lax.all_gather(acts, 'tensor', axis=1, tiled=True)]
    gather x0 -> x3, local copies, waits for them, and re-layouts: none -> 13.7 us  [trace_the_zone(): step_out = step_out[(jnp.arange(world) - raw_out) % world]]
    unnamed x0 -> x1, other arithmetic: none -> 8.24 us
  transfers between devices with their start and end apart: 4 -> 6, of which waited for: 4 -> 5; matrix products, arithmetic and copies ran while one was open for 6% -> 11% of each run, Pallas kernels for 0% -> 0%
where the time goes in v1:
time: 605 us
  waiting for transfers between devices  501 us (83%)
  matrix products  49.6 us (8%)
  other arithmetic  19.5 us (3%)
  local copies, waits for them, and re-layouts  16.6 us (3%)
  between operations  13.2 us (2%)
    reduce_scatter x1, waiting for transfers between devices, shards(): lax.psum_scatter(jnp.einsum('oi,to->it', basis_out, masked, preferred_ele...  160 us
    reduce_scatter x1, waiting for transfers between devices, shards(): summed = lax.psum_scatter(squares, 'dp', scatter_dimension=1, tiled=True)  117 us
    ppermute x1, waiting for transfers between devices, trace_the_zone(): lax.ppermute(val[-1] if val else obj, perm=pages, axis_name=mesh_ax)  115 us
    ppermute x2, waiting for transfers between devices, trace_the_zone(): lax.ppermute(r1[-1] if r1 else obj, axis_name=mesh_ax, perm=trail)  108 us
    dot_general x1, matrix products, shards(): jnp.einsum('oi,to->it', basis_out, masked, preferred_element_type=jnp.flo...  27.5 us
    gather x3, local copies, waits for them, and re-layouts, trace_the_zone(): step_out = step_out[(jnp.arange(world) - raw_out) % world]  13.7 us
    dot_general x2, matrix products, shards(): rotated = jnp.dot(grad_slot, act_slot, preferred_element_type=jnp.float32)  12.2 us
  transfers between devices with their start and end apart: 6, of which 5 were waited for; matrix products, arithmetic and copies ran while one was open for 11% of the time, Pallas kernels for 0%

profile of v1, /device:TPU:0, one launch (start us, length us, event | category | flops | bytes accessed | tf_op | source)
XLA Modules:
  0.0 605.1 jit_solution(10250723935793368517)
XLA Ops:
  6.5 0.0 all-gather.2.cloned.1.call-start
  6.5 0.7 all-gather.2.cloned.1.call-update
  7.3 0.0 reduce-scatter.3.cloned.1.call-start
  7.3 0.8 fusion.13
  8.2 0.8 fusion.14
  9.0 0.1 broadcast_bitcast_fusion
  9.1 27.5 %convolution_bitcast_fusion = f32[8192,512]{0,1:T(8,128)} fusion(bf16[2048,8192]{1,0:T(8,128)(2,1)} %param.8, bf16[512,2048]{1,0:T(8,128)(2,1)} %param.7, pred[512]{0:T(512)(128)(4,1)S(1)} %fusion.9), kind=kOutput, calls=%fused_computation.3 | convolution fusion | flops 17180917760 | bytes 52429312 | tf_op jit(solution)/shard_map/oi,to->it/dot_general | solution.py:49
  36.6 0.0 copy-start.2
  36.6 0.0 reduce-scatter.3.cloned.1.call-update
  36.6 0.0 reduce-scatter.5.cloned.1.call-start
  36.6 1.5 copy-done.2
  38.2 3.0 collective-permute-start
  41.2 2.0 collective-permute-start.2
  43.2 59.7 %collective-permute-done = bf16[512,2048]{1,0:T(8,128)(2,1)} collective-permute-done((bf16[512,2048]{1,0:T(8,128)(2,1)S(1)}, bf16[512,2048]{1,0:T(8,128)(2,1)}, u32[]{:S(2)}, u32[]{:S(2)}) %collective-permute-start) | collective-permute-done | bytes 2097184 | tf_op jit(solution)/shard_map/ppermute | solution.py:22
  103.0 0.0 collective-permute-start.1
  103.0 115.4 %collective-permute-done.2 = bf16[512,2048]{1,0:T(8,128)(2,1)} collective-permute-done((bf16[512,2048]{1,0:T(8,128)(2,1)S(1)}, bf16[512,2048]{1,0:T(8,128)(2,1)}, u32[]{:S(2)}, u32[]{:S(2)}) %collective-permute-start.2) | collective-permute-done | bytes 2097184 | tf_op jit(solution)/shard_map/ppermute | solution.py:24
  218.4 47.8 %collective-permute-done.1 = bf16[512,2048]{1,0:T(8,128)(2,1)} collective-permute-done((bf16[512,2048]{1,0:T(8,128)(2,1)}, bf16[512,2048]{1,0:T(8,128)(2,1)}, u32[]{:S(2)}, u32[]{:S(2)}) %collective-permute-start.1) | collective-permute-done | bytes 2097184 | tf_op jit(solution)/shard_map/ppermute | solution.py:22
  266.3 3.8 pad_maximum_fusion
  270.1 3.7 fusion.18
  273.8 4.9 gather_fusion
  278.8 5.1 gather_fusion.1
  283.8 8.2 %pad_maximum_fusion.1 = bf16[4,512,2048]{2,1,0:T(8,128)(2,1)} fusion(bf16[4,512,1024]{2,1,0:T(8,128)(2,1)} %gather_fusion.1, bf16[4,512,1024]{2,1,0:T(8,128)(2,1)} %gather_fusion), kind=kLoop, calls=%fused_computation.5 | loop fusion | flops 16777216 | bytes 16777216
  292.1 0.0 all-gather.2.cloned.1.call-done
  292.1 9.9 %fusion = bf16[512,2048]{0,1:T(8,128)(2,1)} fusion(bf16[2048,2048]{1,0:T(8,128)(2,1)} %bitcast.17, bf16[512,2048]{1,0:T(8,128)(2,1)} %all-gather.2.cloned.1.call-done), kind=kOutput, calls=%fused_computation.7 | convolution fusion | flops 4296015872 | bytes 12582912 | tf_op jit(solution)/shard_map/dot_general | solution.py:56
  302.0 160.4 %reduce-scatter.3.cloned.1.call-done = f32[2048,512]{0,1:T(8,128)} async-done(((f32[8192,512]{0,1:T(8,128)}), f32[2048,512]{0,1:T(8,128)}) %reduce-scatter.3.cloned.1.call-update) | async-done | bytes 4194320 | tf_op jit(solution)/shard_map/reduce_scatter | solution.py:48
  462.3 0.0 copy-start.1
  462.3 2.6 convert_element_type.9
  465.0 0.0 copy-start
  465.0 1.3 copy-done
  466.3 0.0 copy-done.1
  466.3 2.4 fusion.5
  468.7 9.8 %multiply_add_fusion = f32[2048,2048]{1,0:T(8,128)} fusion(f32[2048,2048]{1,0:T(8,128)S(1)} %fusion.5, bf16[512,2048]{0,1:T(8,128)(2,1)} %fusion, bf16[2048,512]{0,1:T(8,128)(2,1)} %copy-done), kind=kOutput, calls=%fused_computation.2 | convolution fusion | flops 2160066560 | bytes 35651584 | tf_op jit(solution)/shard_map/dot_general | solution.py:63
  478.5 0.0 reduce-scatter.5.cloned.1.call-update
  478.6 117.0 %reduce-scatter.5.cloned.1.call-done = f32[2048,256]{1,0:T(8,128)} async-done(((f32[2048,2048]{1,0:T(8,128)}), f32[2048,256]{1,0:T(8,128)}) %reduce-scatter.5.cloned.1.call-update) | async-done | bytes 2097168 | tf_op jit(solution)/shard_map/reduce_scatter | solution.py:65
  595.6 3.0 broadcast_multiply_fusion
  (5 shorter events, 0.0 us)
Async XLA Ops:
  6.5 285.5 %all-gather.2.cloned.1.call-start = ((), (), s32[]{:S(2)}) async-start(), calls=%async_computation.3 | async-start | bytes 2621440 | tf_op jit(solution)/shard_map/all_gather | solution.py:55
  7.3 455.1 %reduce-scatter.3.cloned.1.call-start = ((), (), s32[]{:S(2)}) async-start(), calls=%async_computation.2 | async-start | bytes 20971520 | tf_op jit(solution)/shard_map/reduce_scatter | solution.py:48
  36.6 1.6 copy-start.2
  36.6 559.0 %reduce-scatter.5.cloned.1.call-start = ((), (), s32[]{:S(2)}) async-start(), calls=%async_computation.4 | async-start | bytes 18874368 | tf_op jit(solution)/shard_map/reduce_scatter | solution.py:65
  38.2 64.8 %collective-permute-start = (bf16[512,2048]{1,0:T(8,128)(2,1)S(1)}, bf16[512,2048]{1,0:T(8,128)(2,1)}, u32[]{:S(2)}, u32[]{:S(2)}) collective-permute-start(bf16[512,2048]{1,0:T(8,128)(2,1)S(1)} %copy-done.2), channel_id=1, source_target_pairs={{0,1},{1,2},{2,3},{3,0},{4,5},{5,6},{6,7},{7,4},{8,9},{9,10},{10,1... | collective-permute-start | bytes 6291464 | tf_op jit(solution)/shard_map/ppermute | solution.py:22
  41.2 177.2 %collective-permute-start.2 = (bf16[512,2048]{1,0:T(8,128)(2,1)S(1)}, bf16[512,2048]{1,0:T(8,128)(2,1)}, u32[]{:S(2)}, u32[]{:S(2)}) collective-permute-start(bf16[512,2048]{1,0:T(8,128)(2,1)S(1)} %copy-done.2), channel_id=1, source_target_pairs={{1,0},{2,1},{3,2},{0,3},{5,4},{6,5},{7,6},{4,7},{9,8},{10,9},{11,1... | collective-permute-start | bytes 6291464 | tf_op jit(solution)/shard_map/ppermute | solution.py:24
  103.0 163.3 %collective-permute-start.1 = (bf16[512,2048]{1,0:T(8,128)(2,1)}, bf16[512,2048]{1,0:T(8,128)(2,1)}, u32[]{:S(2)}, u32[]{:S(2)}) collective-permute-start(bf16[512,2048]{1,0:T(8,128)(2,1)} %collective-permute-done), channel_id=1, source_target_pairs={{0,1},{1,2},{2,3},{3,0},{4,5},{5,6},{6,7},{7,4},{8,9},{9,10},{10,1... | collective-permute-start | bytes 6291464 | tf_op jit(solution)/shard_map/ppermute | solution.py:22
  462.3 4.0 copy-start.1
  465.0 1.3 copy-start
Sparse Core Ops, SparseCore 0:
  8.9 99.7 all-gather.1
  111.1 351.1 reduce-scatter.2
  478.7 116.8 reduce-scatter.4
